TPU v7x, 512 devices: a whole 4x8x8 slice. The times are simulated.
512 devices in a mesh: tm: 64 (over y, x, core), lat: 8 (over z).
Axes of the slice: x: 4, y: 8, z: 8, core: 2. Of those that a mesh axis runs over, the one named last changes fastest.
Arguments:
- trajectory: float32 [128, 3, 128, 320], P('tm', None, 'lat'), may hold values from -6 to 6
- forcing: float32 [128, 3, 128, 320], P('tm', None, 'lat'), may hold values from -6 to 6
- initial_state: float32 [3, 128, 320], P(None, 'lat'), may hold values from -6 to 6
- depth: float32 [128, 320], P('lat'), may hold values from 0.5 to 2
- warm_start: float32 [192, 3, 2, 128, 320], P('tm', None, None, 'lat'), may hold values from -6 to 6
- slot_unit: int32 [64, 3], replicated, may hold values from 0 to 63, as said below
- unit_count: int32 [64], replicated, may hold values from 0 to 3, as said below
Outputs:
- updated: float32 [3, 128, 320, 128], P(None, 'lat', 'tm')
- spectrum: float32 [192, 3, 2, 128, 320], P('tm', None, None, 'lat')
Inputs may be any that keep to these rules, and one draw needn't show every extreme that they name: Owner d holds the pairs slot_unit[d, 0 .. unit_count[d] - 1]; every pair 0 .. 63 is held exactly once over all owners; slots at or past unit_count[d] hold 0. `unit_count`: 8 owners hold 3 pairs, 8 hold 2, 24 hold 1 and the others none; which owners is drawn.
All inputs are finite; a program needn't handle non-finite values.
Results may differ from a plain program's by a relative error of at most 0.0003.
Values sent between devices are 32-bit elements; how exact they have to be, the bound alone decides.
No kernel may reach another device: no remote copies, remote signals or barrier semaphores. Data moves between devices by JAX's collectives and lax.ppermute only.
A program may use at most 64 MiB of HBM per device.

v0:
```python
import math

import jax
import jax.numpy as jnp
from jax import lax
from jax.sharding import PartitionSpec as P

SWEEPS = 6


HALF_COUPLING = 0.125
CORIOLIS = 0.2
FRICTION = 1.0
ALPHA = 0.1
SPREAD = 0.2


def with_halo(cells, sides, width):
    for axis, dim in sides:
        count = lax.axis_size(axis)
        ends = count - 1
        head = lax.slice_in_dim(cells, 0, width, axis=dim)
        tail = lax.slice_in_dim(cells, cells.shape[dim] - width, cells.shape[dim], axis=dim)
        cells = jnp.concatenate(
            [
                lax.ppermute(tail, axis, [(i, (i + 1) % count) for i in range(ends)]),
                cells,
                lax.ppermute(head, axis, [((i + 1) % count, i) for i in range(ends)]),
            ],
            axis=dim,
        )
    return cells


def shifted(value, axis, by):
    size = lax.axis_size(axis)
    pairs = [(i, i + by) for i in range(size) if 0 <= i + by < size]
    return lax.ppermute(value, axis, pairs)


def flux_operator(state, depth, pad_rule, row_mask=None):
    height = state[..., 0:1, :, :, :]
    east = state[..., 1:2, :, :, :]
    north = state[..., 2:3, :, :, :]
    if row_mask is not None:
        height = height * row_mask
    flux = jnp.concatenate([height, depth * east, depth * north], axis=-4)
    padded = pad_rule(flux)
    grad_x = padded[..., 0:1, :, 1:-1, 2:] - padded[..., 0:1, :, 1:-1, :-2]
    grad_y = padded[..., 0:1, :, 2:, 1:-1] - padded[..., 0:1, :, :-2, 1:-1]
    diverge = (
        padded[..., 1:2, :, 1:-1, 2:]
        - padded[..., 1:2, :, 1:-1, :-2]
        + (padded[..., 2:3, :, 2:, 1:-1] - padded[..., 2:3, :, :-2, 1:-1])
    )
    new_height = HALF_COUPLING * diverge
    new_east = HALF_COUPLING * grad_x - CORIOLIS * north
    new_north = HALF_COUPLING * grad_y + CORIOLIS * east
    return jnp.concatenate([new_height, new_east, new_north], axis=-4)


def row_rims(flux):
    rows_done = with_halo(flux, (("lat", 3),), 1)
    return jnp.pad(rows_done, ((0, 0), (0, 0), (0, 0), (0, 0), (1, 1)))


def zero_rim(values):
    widths = [(0, 0)] * (values.ndim - 2) + [(1, 1), (1, 1)]
    return jnp.pad(values, widths)


def to_owners(slots):
    return lax.all_to_all(slots, "tm", split_axis=0, concat_axis=4, tiled=True)


def from_owners(slots):
    return lax.all_to_all(slots, "tm", split_axis=4, concat_axis=0, tiled=True)


def slot_tables(units, filled, step_count):
    index_t = jnp.arange(step_count, dtype=jnp.int32)
    phases = index_t[:, None] * units[None, :] % step_count
    angles = phases.astype(jnp.float32) * (2.0 * math.pi / step_count)
    cosine = jnp.cos(angles)
    sine = jnp.sin(angles)
    parity = (1 - 2 * (index_t % 2)).astype(jnp.float32)
    first = units == 0
    times = index_t.astype(jnp.float32) / step_count
    damping = jnp.exp(times * math.log(ALPHA)) / math.sqrt(step_count)
    growth = jnp.exp(-times * math.log(ALPHA)) / math.sqrt(step_count)
    forward_imag = jnp.where(first[None, :], parity[:, None], -sine)
    forward_table = jnp.stack([cosine, forward_imag], axis=2) * damping[:, None, None]
    weights = jnp.where(first, 1.0, 2.0).astype(jnp.float32)
    inverse_real = cosine * weights[None, :]
    inverse_imag = jnp.where(first[None, :], parity[:, None], -2.0 * sine)
    keep = filled.astype(jnp.float32)[None, :, None]
    inverse_table = jnp.stack([inverse_real, inverse_imag], axis=2) * growth[:, None, None] * keep
    return (forward_table, inverse_table)


def unit_inverse(pair_ids, step_count):
    angles = pair_ids.astype(jnp.float32) * (2.0 * math.pi / step_count)
    ratio = math.exp(math.log(ALPHA) / step_count)
    real_shift = 1.0 + FRICTION - ratio * jnp.cos(angles)
    imag_shift = ratio * jnp.sin(angles)
    denominator = real_shift * real_shift + imag_shift * imag_shift
    real_inv = real_shift / denominator
    imag_inv = -imag_shift / denominator
    is_first = pair_ids == 0
    upper_left = jnp.where(is_first, 1.0 / (1.0 + FRICTION - ratio), real_inv)
    upper_right = jnp.where(is_first, 0.0, -imag_inv)
    lower_left = jnp.where(is_first, 0.0, imag_inv)
    lower_right = jnp.where(is_first, 1.0 / (1.0 + FRICTION + ratio), real_inv)
    return (upper_left, upper_right, lower_left, lower_right)


def apply_inverse(coeffs, values):
    shaped = [c[:, None, None, None] for c in coeffs]
    real_part = values[:, :, 0]
    imag_part = values[:, :, 1]
    new_real = shaped[0] * real_part + shaped[1] * imag_part
    new_imag = shaped[2] * real_part + shaped[3] * imag_part
    return jnp.stack([new_real, new_imag], axis=2)


def chebyshev(source, start, depth, coeffs, row_mask):
    iterate = start
    for sweep in range(SWEEPS):
        weight = 1.0 / (1.0 + SPREAD * math.cos(math.pi * (2 * sweep + 1) / (2 * SWEEPS)))
        flux = flux_operator(iterate, depth, zero_rim, row_mask)
        update = apply_inverse(coeffs, source - flux) - iterate
        iterate = iterate + weight * update
    return iterate


def lat_halo(arrays, width, sent):
    flat = [a.reshape((-1,) + a.shape[-2:]) for a in arrays]
    packed = jnp.concatenate(flat, axis=0)
    rows = packed.shape[1]
    count = lax.axis_size("lat")
    above = lax.ppermute(packed[:, rows - sent :], "lat", [(i, i + 1) for i in range(count - 1)])
    below = lax.ppermute(packed[:, :sent], "lat", [(i + 1, i) for i in range(count - 1)])
    blank = jnp.zeros((packed.shape[0], width - sent, packed.shape[2]), packed.dtype)
    wide = jnp.concatenate([blank, above, packed, below, blank], axis=1)
    out, offset = [], 0
    for a, f in zip(arrays, flat):
        piece = wide[offset : offset + f.shape[0]]
        out.append(piece.reshape(a.shape[:-2] + piece.shape[1:]))
        offset += f.shape[0]
    return out


def body(trajectory, forcing, initial_state, depth, warm_start, slot_unit, unit_count):
    groups = lax.axis_size("tm")
    position = lax.axis_index("tm")
    local_steps = trajectory.shape[0]
    step_count = local_steps * groups
    rows = depth.shape[0]
    lat_count = lax.axis_size("lat")
    lat_pos = lax.axis_index("lat")
    width = 8 * ((SWEEPS + 7) // 8)

    wide_traj, wide_forcing, wide_initial, wide_depth = lat_halo(
        [trajectory, forcing, initial_state, depth], width, SWEEPS
    )
    flux_term = flux_operator(wide_traj[:, :, None], wide_depth, zero_rim)[:, :, 0]
    partial = wide_forcing - ((1.0 + FRICTION) * wide_traj + flux_term)
    keep = width - SWEEPS + 1
    band = slice(keep, rows + 2 * width - keep)
    band_traj = wide_traj[:, :, band]
    band_part = partial[:, :, band]
    payload = jnp.concatenate(
        [
            wide_traj[0, :, width : width + rows],
            band_traj[1],
            band_part[0],
            band_part[1] + band_traj[0],
        ],
        axis=1,
    )
    outgoing_rows, warm_start = lax.optimization_barrier((payload[None], warm_start))
    (wide_start,) = lat_halo([warm_start], width, SWEEPS)
    moved = lax.all_to_all(outgoing_rows, "tm", split_axis=3, concat_axis=0, tiled=True)
    band_rows = band_traj.shape[2]
    first = moved[:, :, :rows]
    second = moved[:, :, rows : rows + band_rows]
    even_part = moved[:, :, rows + band_rows : rows + 2 * band_rows]
    odd_resid = moved[:, :, rows + 2 * band_rows :]
    col_count = moved.shape[3]
    initial_cols = lax.dynamic_slice_in_dim(
        wide_initial[:, band], position * col_count, col_count, axis=2
    )
    previous = jnp.concatenate([initial_cols[None], second[:-1]], axis=0)
    resid_cols = jnp.stack([even_part + previous, odd_resid], axis=1)
    resid_cols = resid_cols.reshape((-1,) + resid_cols.shape[2:])
    inner = width - keep
    state_cols = jnp.stack([first, second[:, :, inner : inner + rows]], axis=1)
    state_cols = jnp.transpose(state_cols.reshape((-1,) + state_cols.shape[2:]), (1, 2, 3, 0))

    flat_units = slot_unit.reshape(-1)
    slot_total = slot_unit.shape[1]
    filled = (jnp.arange(slot_total, dtype=jnp.int32)[None, :] < unit_count[:, None]).reshape(-1)
    forward_table, inverse_table = slot_tables(flat_units, filled, step_count)

    outgoing = jnp.einsum(
        "tsp,tfyx->spfyx", forward_table, resid_cols, precision=lax.Precision.HIGH
    )
    pads = ((0, 0), (0, 0), (0, 0), (keep, keep), (0, 0))
    wide_source = jnp.pad(jnp.transpose(to_owners(outgoing), (0, 2, 1, 3, 4)), pads)

    own_units = lax.dynamic_index_in_dim(slot_unit, position, 0, keepdims=False)
    own_filled = lax.dynamic_index_in_dim(filled.reshape(groups, -1), position, 0, keepdims=False)
    coeffs = unit_inverse(own_units, step_count)

    global_row = lat_pos * rows - width + jnp.arange(rows + 2 * width, dtype=jnp.int32)
    row_mask = ((global_row >= 0) & (global_row < rows * lat_count)).astype(jnp.float32)
    solved = chebyshev(wide_source, wide_start, wide_depth, coeffs, row_mask[:, None])
    solved = solved[:, :, :, width : width + rows]
    spectrum = jnp.where(own_filled[:, None, None, None, None], solved, 0.0)

    turned = jnp.transpose(solved, (0, 2, 1, 3, 4))
    flat_solved = turned.reshape((1, -1, turned.shape[-1]))
    solved_cols = lax.all_to_all(flat_solved, "tm", split_axis=2, concat_axis=0, tiled=True)
    solved_cols = solved_cols.reshape(
        (groups * turned.shape[0],) + turned.shape[1:4] + (solved_cols.shape[-1],)
    )
    corr = jnp.einsum(
        "spfyx,tsp->fyxt", solved_cols, inverse_table, precision=lax.Precision.HIGH
    )
    updated = state_cols + corr
    return (updated, spectrum)


def solution(mesh):
    return jax.shard_map(
        body,
        mesh=mesh,
        in_specs=(
            P("tm", None, "lat", None),
            P("tm", None, "lat", None),
            P(None, "lat", None),
            P("lat", None),
            P("tm", None, None, "lat", None),
            P(),
            P(),
        ),
        out_specs=(P(None, "lat", "tm", None), P("tm", None, None, "lat", None)),
        check_vma=False,
    )
```

profile of v0, /device:TPU:193, one launch (start us, length us, event | category | flops | bytes accessed | tf_op | source)
XLA Modules:
  0.0 141.9 jit_solution(17133459229797222004)
XLA Ops:
  0.6 1.1 pad_maximum_fusion.3
  1.7 1.9 %collective-permute-start.1 = (f32[16,6,320]{2,1,0:T(8,128)S(1)}, f32[16,6,320]{2,1,0:T(8,128)S(1)}, u32[]{:S(2)}, u32[]{:S(2)}) collective-permute-start(f32[16,6,320]{2,1,0:T(8,128)S(1)} %get-tuple-element.85), channel_id=1, source_target_pairs={{1,0},{2,1},{3,2},{4,3},{5,4},{6,5},{7,6},{9,8},{10,9},{11,10},{12... | collective-permute-start | bytes 368648 | tf_op jit(solution)/shard_map/ppermute | solution.py:142
  3.7 5.2 %collective-permute-start = (f32[16,6,320]{2,1,0:T(8,128)S(1)}, f32[16,6,320]{2,1,0:T(8,128)S(1)}, u32[]{:S(2)}, u32[]{:S(2)}) collective-permute-start(f32[16,6,320]{2,1,0:T(8,128)S(1)} %get-tuple-element.86), channel_id=1, source_target_pairs={{0,1},{1,2},{2,3},{3,4},{4,5},{5,6},{6,7},{8,9},{9,10},{10,11},{11... | collective-permute-start | bytes 368648 | tf_op jit(solution)/shard_map/ppermute | solution.py:141
  9.6 1.9 %collective-permute-done.1 = f32[16,6,320]{2,1,0:T(8,128)S(1)} collective-permute-done((f32[16,6,320]{2,1,0:T(8,128)S(1)}, f32[16,6,320]{2,1,0:T(8,128)S(1)}, u32[]{:S(2)}, u32[]{:S(2)}) %collective-permute-start.1) | collective-permute-done | bytes 122912 | tf_op jit(solution)/shard_map/ppermute | solution.py:142
  11.6 0.9 collective-permute-done
  13.5 1.2 copy.337
  14.7 11.7 %all-to-all-start = ((f32[1,3,94,320]{2,0,1,3:T(1,128)}), f32[1,3,94,320]{2,0,1,3:T(1,128)S(1)}, u32[]{:S(2)}, u32[]{:S(2)}) async-start(f32[1,3,94,320]{2,0,1,3:T(1,128)} %copy.337), calls=%async_computation | async-start | bytes 983040 | tf_op jit(solution)/shard_map/all_to_all | solution.py:183
  26.4 1.2 multiply_select_fusion
  27.8 15.5 %all-to-all-done = f32[1,3,94,320]{2,0,1,3:T(1,128)S(1)} async-done(((f32[1,3,94,320]{2,0,1,3:T(1,128)}), f32[1,3,94,320]{2,0,1,3:T(1,128)S(1)}, u32[]{:S(2)}, u32[]{:S(2)}) %all-to-all-start) | async-done | bytes 360992 | tf_op jit(solution)/shard_map/all_to_all | solution.py:183
  43.4 0.3 copy.338
  44.0 0.3 fusion.21
  44.4 0.8 copy.351
  45.1 2.1 %fusion.67 = f32[192,2,3,26,5]{0,3,4,2,1:T(8,128)} fusion(f32[128,3,26,5,1]{2,0,3,1,4:T(8,128)S(1)} %bitcast.101, f32[128,192,1]{0,1,2:T(8,128)S(1)} %get-tuple-element.95, f32[128,192,1]{0,1,2:T(8,128)S(1)} %get-tuple-element.99, f32[128]{0:T(128)S(1)} %exponential_multiply_fusion.1), kind=kOutput, calls=%fused_computation.163 | convolution fusion | flops 115113984 | bytes 995840 | tf_op jit(solution)/shard_map/tsp,tfyx->spfyx/dot_general | solution.py:205
  47.2 3.9 %copy.353 = f32[192,2,3,26,5]{3,1,4,2,0:T(2,128)S(1)} copy(f32[192,2,3,26,5]{0,3,4,2,1:T(8,128)} %fusion.67) | data formatting | bytes 1198080 | tf_op jit(solution)/shard_map/tsp,tfyx->spfyx/dot_general | solution.py:205
  51.1 4.2 %reshape.482 = f32[64,1,2340]{2,1,0:T(1,128)} reshape(f32[192,3,5,2,26]{4,3,2,1,0:T(2,128)S(1)} %bitcast.93) | data formatting | bytes 1198080
  55.3 5.8 %all-to-all-start.1 = ((f32[64,1,2340]{2,1,0:T(1,128)}), f32[64,1,2340]{2,1,0:T(1,128)S(1)}, u32[]{:S(2)}, u32[]{:S(2)}) async-start(f32[64,1,2340]{2,1,0:T(1,128)} %reshape.482), calls=%async_computation.1 | async-start | bytes 1245184 | tf_op jit(solution)/shard_map/all_to_all | solution.py:73
  61.3 5.3 %collective-permute-start.2 = (f32[18,6,320]{2,0,1:T(8,128)S(1)}, f32[18,6,320]{2,0,1:T(8,128)S(1)}, u32[]{:S(2)}, u32[]{:S(2)}) collective-permute-start(f32[18,6,320]{2,0,1:T(8,128)S(1)} %copy.370), channel_id=1, source_target_pairs={{0,1},{1,2},{2,3},{3,4},{4,5},{5,6},{6,7},{8,9},{9,10},{10,11},{11... | collective-permute-start | bytes 414728 | tf_op jit(solution)/shard_map/ppermute | solution.py:141
  66.6 2.1 %collective-permute-start.3 = (f32[18,6,320]{2,0,1:T(8,128)S(1)}, f32[18,6,320]{2,0,1:T(8,128)S(1)}, u32[]{:S(2)}, u32[]{:S(2)}) collective-permute-start(f32[18,6,320]{2,0,1:T(8,128)S(1)} %copy.371), channel_id=1, source_target_pairs={{1,0},{2,1},{3,2},{4,3},{5,4},{6,5},{7,6},{9,8},{10,9},{11,10},{12... | collective-permute-start | bytes 414728 | tf_op jit(solution)/shard_map/ppermute | solution.py:142
  68.8 2.2 %collective-permute-done.2 = f32[18,6,320]{2,0,1:T(8,128)S(1)} collective-permute-done((f32[18,6,320]{2,0,1:T(8,128)S(1)}, f32[18,6,320]{2,0,1:T(8,128)S(1)}, u32[]{:S(2)}, u32[]{:S(2)}) %collective-permute-start.2) | collective-permute-done | bytes 138272 | tf_op jit(solution)/shard_map/ppermute | solution.py:141
  71.0 5.0 %collective-permute-done.3 = f32[18,6,320]{2,0,1:T(8,128)S(1)} collective-permute-done((f32[18,6,320]{2,0,1:T(8,128)S(1)}, f32[18,6,320]{2,0,1:T(8,128)S(1)}, u32[]{:S(2)}, u32[]{:S(2)}) %collective-permute-start.3) | collective-permute-done | bytes 138272 | tf_op jit(solution)/shard_map/ppermute | solution.py:142
  76.4 0.4 select_maximum_fusion.10
  76.8 1.3 fusion.61
  78.0 2.8 %all-to-all-done.1 = f32[64,1,2340]{2,1,0:T(1,128)S(1)} async-done(((f32[64,1,2340]{2,1,0:T(1,128)}), f32[64,1,2340]{2,1,0:T(1,128)S(1)}, u32[]{:S(2)}, u32[]{:S(2)}) %all-to-all-start.1) | async-done | bytes 599072 | tf_op jit(solution)/shard_map/all_to_all | solution.py:73
  80.8 0.5 broadcast.800
  81.3 2.0 %reduce.8 = f32[64,2340]{1,0:T(8,128)S(1)} reduce(f32[64,1,2340]{2,1,0:T(1,128)S(1)} %all-to-all-done.1, f32[]{:T(128)} %broadcast.800), dimensions={1}, to_apply=%all_to_all.41.reduce_sub_computation | reduce | bytes 1198084 | tf_op jit(solution)/shard_map/all_to_all | solution.py:73
  83.4 3.6 %reshape.483 = f32[192,3,5,2,26]{4,3,2,1,0:T(2,128)} reshape(f32[64,2340]{1,0:T(8,128)S(1)} %reduce.8) | data formatting | bytes 1198080
  87.0 4.6 %copy.354 = f32[3,2,3,26,64,5]{3,1,5,4,2,0:T(2,128)} copy(f32[3,2,3,26,64,5]{3,1,5,2,0,4:T(2,128)} %bitcast.94) | data formatting | bytes 1198080 | tf_op jit(solution)/shard_map/all_to_all | solution.py:73
  91.6 4.7 %copy.355 = f32[3,2,3,26,320]{4,3,1,2,0:T(8,128)S(1)} copy(f32[3,2,3,26,320]{3,1,4,2,0:T(2,128)} %bitcast.95) | data formatting | bytes 1198080 | tf_op jit(solution)/shard_map/all_to_all | solution.py:73
  97.0 0.4 select_maximum_fusion.8
  97.3 0.6 fusion.55
  98.6 0.4 select_maximum_fusion.6
  99.0 0.6 fusion.49
  99.9 0.4 fusion.16
  100.4 0.4 select_maximum_fusion.4
  100.8 0.6 fusion.43
  101.7 0.5 fusion.18
  102.3 0.4 select_maximum_fusion.2
  102.7 0.6 fusion.37
  103.7 0.6 fusion.20
  104.4 0.4 select_maximum_fusion
  104.7 0.6 fusion.31
  105.7 0.9 broadcast_select_fusion
  106.6 1.2 copy.357
  107.8 8.7 %all-to-all-start.2 = ((f32[1,288,320]{1,0,2:T(1,128)}), f32[1,288,320]{1,0,2:T(1,128)S(1)}, u32[]{:S(2)}, u32[]{:S(2)}) async-start(f32[1,288,320]{1,0,2:T(1,128)} %copy.357), calls=%async_computation.2 | async-start | bytes 983040 | tf_op jit(solution)/shard_map/all_to_all | solution.py:223
  117.0 0.8 copy.340
  118.0 15.5 %all-to-all-done.2 = f32[1,288,320]{1,0,2:T(1,128)S(1)} async-done(((f32[1,288,320]{1,0,2:T(1,128)}), f32[1,288,320]{1,0,2:T(1,128)S(1)}, u32[]{:S(2)}, u32[]{:S(2)}) %all-to-all-start.2) | async-done | bytes 368672 | tf_op jit(solution)/shard_map/all_to_all | solution.py:223
  133.6 3.0 %reshape.468 = f32[192,2,3,16,5]{3,2,1,0,4:T(4,128)} reshape(f32[64,1,288,5]{2,0,3,1:T(8,128)S(1)} %copy.358) | data formatting | bytes 737280 | tf_op jit(solution)/shard_map/reshape | solution.py:224
  136.7 5.2 %fusion.5 = f32[3,16,5,128]{3,1,2,0:T(8,128)} fusion(f32[192,2,3,16,5]{3,2,1,0,4:T(4,128)} %reshape.468, f32[128,192,1]{0,1,2:T(8,128)S(1)} %copy-done.4, f32[128,192,1]{0,1,2:T(8,128)S(1)} %copy-done.5, f32[128,3,16,5]{0,2,3,1:T(8,128)S(1)} %copy.341, f32[192]{0:T(256)S(1)} %reshape.473, f32[128]{0:T(128)S(1)} %exponential_multiply_fusion), kind=kOutput, calls=%fused_computation.7 | convolution fusion | flops 70957056 | bytes 812288 | tf_op jit(solution)/shard_map/spfyx,tsp->fyxt/dot_general | solution.py:227
  (83 shorter events, 6.5 us)
Async XLA Ops:
  0.6 8.3 %copy-start.8 = (s32[64,3]{0,1:T(4,128)S(1)}, s32[64,3]{0,1:T(4,128)}, u32[]{:S(2)}) copy-start(s32[64,3]{0,1:T(4,128)} %param.12) | copy-start | bytes 2308
  1.7 9.8 %collective-permute-start.1 = (f32[16,6,320]{2,1,0:T(8,128)S(1)}, f32[16,6,320]{2,1,0:T(8,128)S(1)}, u32[]{:S(2)}, u32[]{:S(2)}) collective-permute-start(f32[16,6,320]{2,1,0:T(8,128)S(1)} %get-tuple-element.85), channel_id=1, source_target_pairs={{1,0},{2,1},{3,2},{4,3},{5,4},{6,5},{7,6},{9,8},{10,9},{11,10},{12... | collective-permute-start | bytes 368648 | tf_op jit(solution)/shard_map/ppermute | solution.py:142
  3.7 8.8 %collective-permute-start = (f32[16,6,320]{2,1,0:T(8,128)S(1)}, f32[16,6,320]{2,1,0:T(8,128)S(1)}, u32[]{:S(2)}, u32[]{:S(2)}) collective-permute-start(f32[16,6,320]{2,1,0:T(8,128)S(1)} %get-tuple-element.86), channel_id=1, source_target_pairs={{0,1},{1,2},{2,3},{3,4},{4,5},{5,6},{6,7},{8,9},{9,10},{10,11},{11... | collective-permute-start | bytes 368648 | tf_op jit(solution)/shard_map/ppermute | solution.py:141
  13.4 13.0 %copy-start.9 = (s32[64]{0:T(128)S(1)}, s32[64]{0:T(128)}, u32[]{:S(2)}) copy-start(s32[64]{0:T(128)} %param.13) | copy-start | bytes 772
  13.4 14.2 %copy-start.2 = (f32[2,3,16,320]{3,2,1,0:T(8,128)S(1)}, f32[2,3,16,320]{3,2,1,0:T(8,128)}, u32[]{:S(2)}) copy-start(f32[2,3,16,320]{3,2,1,0:T(8,128)} %param.8) | copy-start | bytes 368644
  13.4 14.2 %copy-start.3 = (f32[2,3,16,320]{3,2,1,0:T(8,128)S(1)}, f32[2,3,16,320]{3,2,1,0:T(8,128)}, u32[]{:S(2)}) copy-start(f32[2,3,16,320]{3,2,1,0:T(8,128)} %param.7) | copy-start | bytes 368644
  13.4 14.2 %copy-start.6 = (f32[3,16,320]{2,1,0:T(8,128)S(1)}, f32[3,16,320]{2,1,0:T(8,128)}, u32[]{:S(2)}) copy-start(f32[3,16,320]{2,1,0:T(8,128)} %param.9) | copy-start | bytes 184324
  13.4 14.2 %copy-start.7 = (f32[16,320]{1,0:T(8,128)S(1)}, f32[16,320]{1,0:T(8,128)}, u32[]{:S(2)}) copy-start(f32[16,320]{1,0:T(8,128)} %param.10) | copy-start | bytes 61444
  14.7 28.7 %all-to-all-start = ((f32[1,3,94,320]{2,0,1,3:T(1,128)}), f32[1,3,94,320]{2,0,1,3:T(1,128)S(1)}, u32[]{:S(2)}, u32[]{:S(2)}) async-start(f32[1,3,94,320]{2,0,1,3:T(1,128)} %copy.337), calls=%async_computation | async-start | bytes 983040 | tf_op jit(solution)/shard_map/all_to_all | solution.py:183
  55.3 5.9 %copy-start = (f32[3,3,2,16,320]{4,3,2,1,0:T(8,128)S(1)}, f32[3,3,2,16,320]{4,3,2,1,0:T(8,128)}, u32[]{:S(2)}) copy-start(f32[3,3,2,16,320]{4,3,2,1,0:T(8,128)} %param.11) | copy-start | bytes 1105924
  55.3 25.5 %all-to-all-start.1 = ((f32[64,1,2340]{2,1,0:T(1,128)}), f32[64,1,2340]{2,1,0:T(1,128)S(1)}, u32[]{:S(2)}, u32[]{:S(2)}) async-start(f32[64,1,2340]{2,1,0:T(1,128)} %reshape.482), calls=%async_computation.1 | async-start | bytes 1245184 | tf_op jit(solution)/shard_map/all_to_all | solution.py:73
  61.3 9.7 %collective-permute-start.2 = (f32[18,6,320]{2,0,1:T(8,128)S(1)}, f32[18,6,320]{2,0,1:T(8,128)S(1)}, u32[]{:S(2)}, u32[]{:S(2)}) collective-permute-start(f32[18,6,320]{2,0,1:T(8,128)S(1)} %copy.370), channel_id=1, source_target_pairs={{0,1},{1,2},{2,3},{3,4},{4,5},{5,6},{6,7},{8,9},{9,10},{10,11},{11... | collective-permute-start | bytes 414728 | tf_op jit(solution)/shard_map/ppermute | solution.py:141
  66.6 9.3 %collective-permute-start.3 = (f32[18,6,320]{2,0,1:T(8,128)S(1)}, f32[18,6,320]{2,0,1:T(8,128)S(1)}, u32[]{:S(2)}, u32[]{:S(2)}) collective-permute-start(f32[18,6,320]{2,0,1:T(8,128)S(1)} %copy.371), channel_id=1, source_target_pairs={{1,0},{2,1},{3,2},{4,3},{5,4},{6,5},{7,6},{9,8},{10,9},{11,10},{12... | collective-permute-start | bytes 414728 | tf_op jit(solution)/shard_map/ppermute | solution.py:142
  91.6 4.7 %copy-start.1 = (f32[3,1,2,32,320]{4,3,2,1,0:T(8,128)S(1)}, f32[3,1,2,32,320]{4,3,2,1,0:T(8,128)}, u32[]{:S(2)}) copy-start(f32[3,1,2,32,320]{4,3,2,1,0:T(8,128)} %get-tuple-element.44) | copy-start | bytes 737284
  107.8 25.8 %all-to-all-start.2 = ((f32[1,288,320]{1,0,2:T(1,128)}), f32[1,288,320]{1,0,2:T(1,128)S(1)}, u32[]{:S(2)}, u32[]{:S(2)}) async-start(f32[1,288,320]{1,0,2:T(1,128)} %copy.357), calls=%async_computation.2 | async-start | bytes 983040 | tf_op jit(solution)/shard_map/all_to_all | solution.py:223
  133.6 3.0 %copy-start.4 = (f32[128,192,1]{0,1,2:T(8,128)S(1)}, f32[128,192,1]{0,1,2:T(8,128)}, u32[]{:S(2)}) copy-start(f32[128,192,1]{0,1,2:T(8,128)} %get-tuple-element.94) | copy-start | bytes 294916
  133.6 3.0 %copy-start.5 = (f32[128,192,1]{0,1,2:T(8,128)S(1)}, f32[128,192,1]{0,1,2:T(8,128)}, u32[]{:S(2)}) copy-start(f32[128,192,1]{0,1,2:T(8,128)} %get-tuple-element.98) | copy-start | bytes 294916
where the time goes:
time: 143 us; the launch traced here: 142 us
  waiting for transfers between devices  43.8 us (31%)
  starting transfers between devices  40.8 us (29%)
  local copies, waits for them, and re-layouts  30.9 us (22%)
  other arithmetic  17.7 us (12%)
  matrix products  7.3 us (5%)
    all_to_all x1, waiting for transfers between devices, body(): lax.all_to_all(flat_solved, 'tm', split_axis=2, concat_axis=0, tiled=True)  15.5 us
    all_to_all x1, waiting for transfers between devices, body(): lax.all_to_all(outgoing_rows, 'tm', split_axis=3, concat_axis=0, tiled=True)  15.5 us
    all_to_all x1, starting transfers between devices, body(): lax.all_to_all(outgoing_rows, 'tm', split_axis=3, concat_axis=0, tiled=True)  11.7 us
    ppermute x2, starting transfers between devices, lat_halo(): lax.ppermute(packed[:, rows - sent:], 'lat', [(i, i + 1) for i in range(c...  10.5 us
    all_to_all x3, local copies, waits for them, and re-layouts, to_owners(): return lax.all_to_all(slots, 'tm', split_axis=0, concat_axis=4, tiled=True)  9.83 us
    all_to_all x1, starting transfers between devices, body(): lax.all_to_all(flat_solved, 'tm', split_axis=2, concat_axis=0, tiled=True)  8.75 us
    unnamed x25, local copies, waits for them, and re-layouts  8.05 us
    ppermute x2, waiting for transfers between devices, lat_halo(): lax.ppermute(packed[:, :sent], 'lat', [(i + 1, i) for i in range(count -...  6.9 us
  transfers between devices with their start and end apart: 7, of which 7 were waited for; matrix products, arithmetic and copies ran while one was open for 4% of the time, Pallas kernels for 0%

commit v1 on v0

--- a/solution.py
+++ b/solution.py
@@ -203,10 +203,15 @@
     forward_table, inverse_table = slot_tables(flat_units, filled, step_count)
 
     outgoing = jnp.einsum(
-        "tsp,tfyx->spfyx", forward_table, resid_cols, precision=lax.Precision.HIGH
+        "tsp,tfyx->fpyxs", forward_table, resid_cols, precision=lax.Precision.HIGH
     )
     pads = ((0, 0), (0, 0), (0, 0), (keep, keep), (0, 0))
-    wide_source = jnp.pad(jnp.transpose(to_owners(outgoing), (0, 2, 1, 3, 4)), pads)
+    received = lax.all_to_all(
+        outgoing.reshape((1, -1, outgoing.shape[-1])), "tm", split_axis=2, concat_axis=0, tiled=True
+    )
+    received = received.reshape((groups,) + outgoing.shape[:4] + (-1,))
+    owned = jnp.transpose(received, (5, 1, 2, 3, 0, 4))
+    wide_source = jnp.pad(owned.reshape(owned.shape[:4] + (-1,)), pads)
 
     own_units = lax.dynamic_index_in_dim(slot_unit, position, 0, keepdims=False)
     own_filled = lax.dynamic_index_in_dim(filled.reshape(groups, -1), position, 0, keepdims=False)

time: 143 us -> 135 us (0.944)
  local copies, waits for them, and re-layouts: 30.9 us -> 26 us
    reshape x0 -> x4, local copies, waits for them, and re-layouts: none -> 8.14 us  [the longest x1 4.54 us: body(): wide_source = jnp.pad(owned.reshape(owned.shape[:4] + (-1,)), pads)]
    all_to_all x3 -> x1, local copies, waits for them, and re-layouts: 9.83 us -> 1.9 us  [body(): lax.all_to_all(outgoing.reshape((1, -1, outgoing.shape[-1])), 'tm', split...]
    unnamed x25 -> x29, local copies, waits for them, and re-layouts: 8.05 us -> 1.16 us
    transpose x0 -> x2, local copies, waits for them, and re-layouts: none -> 5.07 us  [the longest x1 4.58 us: body(): owned = jnp.transpose(received, (5, 1, 2, 3, 0, 4))]
    dot_general x1 -> x0, local copies, waits for them, and re-layouts: 3.9 us -> none  [body(): jnp.einsum('tsp,tfyx->spfyx', forward_table, resid_cols, precision=lax.Pr...]
    all_to_all x1 -> x0, other arithmetic: 2.04 us -> none  [to_owners(): return lax.all_to_all(slots, 'tm', split_axis=0, concat_axis=4, tiled=True)]
  transfers between devices with their start and end apart: 7 -> 7, of which waited for: 7 -> 7; matrix products, arithmetic and copies ran while one was open for 4% -> 6% of each run, Pallas kernels for 0% -> 0%
where the time goes in v1:
time: 135 us
  waiting for transfers between devices  43.3 us (32%)
  starting transfers between devices  40.2 us (30%)
  local copies, waits for them, and re-layouts  26 us (19%)
  other arithmetic  17 us (13%)
  matrix products  7 us (5%)
  between operations  1.37 us (1%)
    all_to_all x1, waiting for transfers between devices, body(): lax.all_to_all(outgoing_rows, 'tm', split_axis=3, concat_axis=0, tiled=True)  15.6 us
    all_to_all x1, waiting for transfers between devices, body(): lax.all_to_all(flat_solved, 'tm', split_axis=2, concat_axis=0, tiled=True)  15.5 us
    all_to_all x1, starting transfers between devices, body(): lax.all_to_all(outgoing_rows, 'tm', split_axis=3, concat_axis=0, tiled=True)  11.7 us
    ppermute x2, starting transfers between devices, lat_halo(): lax.ppermute(packed[:, rows - sent:], 'lat', [(i, i + 1) for i in range(c...  10.5 us
    all_to_all x1, starting transfers between devices, body(): lax.all_to_all(flat_solved, 'tm', split_axis=2, concat_axis=0, tiled=True)  8.25 us
    ppermute x2, waiting for transfers between devices, lat_halo(): lax.ppermute(packed[:, :sent], 'lat', [(i + 1, i) for i in range(count -...  6.9 us
    all_to_all x1, starting transfers between devices, body(): lax.all_to_all(outgoing.reshape((1, -1, outgoing.shape[-1])), 'tm', split...  5.69 us
    dot_general x1, matrix products, body(): jnp.einsum('spfyx,tsp->fyxt', solved_cols, inverse_table, precision=lax.P...  5.24 us
  transfers between devices with their start and end apart: 7, of which 7 were waited for; matrix products, arithmetic and copies ran while one was open for 6% of the time, Pallas kernels for 0%

profile of v1, /device:TPU:193, one launch (start us, length us, event | category | flops | bytes accessed | tf_op | source)
XLA Modules:
  0.0 134.8 jit_solution(6555295376159340956)
XLA Ops:
  0.6 1.1 pad_maximum_fusion.3
  1.7 1.9 %collective-permute-start.1 = (f32[16,6,320]{2,1,0:T(8,128)S(1)}, f32[16,6,320]{2,1,0:T(8,128)S(1)}, u32[]{:S(2)}, u32[]{:S(2)}) collective-permute-start(f32[16,6,320]{2,1,0:T(8,128)S(1)} %get-tuple-element.85), channel_id=1, source_target_pairs={{1,0},{2,1},{3,2},{4,3},{5,4},{6,5},{7,6},{9,8},{10,9},{11,10},{12... | collective-permute-start | bytes 368648 | tf_op jit(solution)/shard_map/ppermute | solution.py:142
  3.7 5.2 %collective-permute-start = (f32[16,6,320]{2,1,0:T(8,128)S(1)}, f32[16,6,320]{2,1,0:T(8,128)S(1)}, u32[]{:S(2)}, u32[]{:S(2)}) collective-permute-start(f32[16,6,320]{2,1,0:T(8,128)S(1)} %get-tuple-element.86), channel_id=1, source_target_pairs={{0,1},{1,2},{2,3},{3,4},{4,5},{5,6},{6,7},{8,9},{9,10},{10,11},{11... | collective-permute-start | bytes 368648 | tf_op jit(solution)/shard_map/ppermute | solution.py:141
  9.6 1.9 %collective-permute-done.1 = f32[16,6,320]{2,1,0:T(8,128)S(1)} collective-permute-done((f32[16,6,320]{2,1,0:T(8,128)S(1)}, f32[16,6,320]{2,1,0:T(8,128)S(1)}, u32[]{:S(2)}, u32[]{:S(2)}) %collective-permute-start.1) | collective-permute-done | bytes 122912 | tf_op jit(solution)/shard_map/ppermute | solution.py:142
  11.6 0.9 collective-permute-done
  13.5 1.2 copy.345
  14.7 11.7 %all-to-all-start = ((f32[1,3,94,320]{2,0,1,3:T(1,128)}), f32[1,3,94,320]{2,0,1,3:T(1,128)S(1)}, u32[]{:S(2)}, u32[]{:S(2)}) async-start(f32[1,3,94,320]{2,0,1,3:T(1,128)} %copy.345), calls=%async_computation | async-start | bytes 983040 | tf_op jit(solution)/shard_map/all_to_all | solution.py:183
  26.4 0.7 iota_compare_fusion.8
  27.1 0.5 multiply_select_fusion
  27.8 15.6 %all-to-all-done = f32[1,3,94,320]{2,0,1,3:T(1,128)S(1)} async-done(((f32[1,3,94,320]{2,0,1,3:T(1,128)}), f32[1,3,94,320]{2,0,1,3:T(1,128)S(1)}, u32[]{:S(2)}, u32[]{:S(2)}) %all-to-all-start) | async-done | bytes 360992 | tf_op jit(solution)/shard_map/all_to_all | solution.py:183
  44.4 0.8 copy.358
  45.1 1.8 %convolution_bitcast_fusion = f32[3,2,26,5,192]{4,2,1,3,0:T(8,128)S(1)} fusion(f32[128,3,26,5,1]{2,0,4,3,1:T(8,128)S(1)} %bitcast.98, f32[128,192,1]{0,1,2:T(8,128)S(1)} %get-tuple-element.95, f32[128,192,1]{0,1,2:T(8,128)S(1)} %get-tuple-element.99, f32[128]{0:T(128)S(1)} %exponential_multiply_fusion.1), kind=kOutput, calls=%fused_computation.6 | convolution fusion | flops 115113984 | bytes 995840 | tf_op jit(solution)/shard_map/tsp,tfyx->fpyxs/dot_general | solution.py:205
  46.9 0.5 copy.361
  47.6 2.0 %copy.362 = f32[1,780,192]{1,0,2:T(1,128)} copy(f32[1,780,192]{2,1,0:T(8,128)S(1)} %reshape.477) | data formatting | bytes 1198080 | tf_op jit(solution)/shard_map/reshape | solution.py:210
  49.5 5.7 %all-to-all-start.1 = ((f32[1,780,192]{1,0,2:T(1,128)}), f32[1,780,192]{1,0,2:T(1,128)S(1)}, u32[]{:S(2)}, u32[]{:S(2)}) async-start(f32[1,780,192]{1,0,2:T(1,128)} %copy.362), calls=%async_computation.1 | async-start | bytes 1376256 | tf_op jit(solution)/shard_map/all_to_all | solution.py:209
  55.4 5.3 %collective-permute-start.2 = (f32[18,6,320]{2,0,1:T(8,128)S(1)}, f32[18,6,320]{2,0,1:T(8,128)S(1)}, u32[]{:S(2)}, u32[]{:S(2)}) collective-permute-start(f32[18,6,320]{2,0,1:T(8,128)S(1)} %copy.381), channel_id=1, source_target_pairs={{0,1},{1,2},{2,3},{3,4},{4,5},{5,6},{6,7},{8,9},{9,10},{10,11},{11... | collective-permute-start | bytes 414728 | tf_op jit(solution)/shard_map/ppermute | solution.py:141
  60.7 2.1 %collective-permute-start.3 = (f32[18,6,320]{2,0,1:T(8,128)S(1)}, f32[18,6,320]{2,0,1:T(8,128)S(1)}, u32[]{:S(2)}, u32[]{:S(2)}) collective-permute-start(f32[18,6,320]{2,0,1:T(8,128)S(1)} %copy.382), channel_id=1, source_target_pairs={{1,0},{2,1},{3,2},{4,3},{5,4},{6,5},{7,6},{9,8},{10,9},{11,10},{12... | collective-permute-start | bytes 414728 | tf_op jit(solution)/shard_map/ppermute | solution.py:142
  62.8 0.5 and_convert_fusion
  63.4 0.6 fusion.99
  64.0 1.1 collective-permute-done.2
  65.1 5.0 %collective-permute-done.3 = f32[18,6,320]{2,0,1:T(8,128)S(1)} collective-permute-done((f32[18,6,320]{2,0,1:T(8,128)S(1)}, f32[18,6,320]{2,0,1:T(8,128)S(1)}, u32[]{:S(2)}, u32[]{:S(2)}) %collective-permute-start.3) | collective-permute-done | bytes 138272 | tf_op jit(solution)/shard_map/ppermute | solution.py:142
  70.4 0.7 slice_multiply_fusion.17
  71.1 0.4 select_maximum_fusion.10
  71.5 1.4 %fusion.61 = (f32[3,1,2,32,320]{4,3,2,1,0:T(8,128)}, f32[3,1,2,32,320]{4,3,2,1,0:T(8,128)}, f32[3,1,2,32,320]{4,3,2,1,0:T(8,128)}) fusion(f32[3,3,2,34,322]{4,3,2,1,0:T(8,128)S(1)} %select_maximum_fusion.10, f32[3,3,2,32,320]{4,3,2,1,0:T(8,128)S(1)} %concatenate.72), kind=kLoop, calls=%fused_computation.140 | loop fusion | flops 737280 | bytes 3194880 | tf_op jit(solution)/shard_map/sub | solution.py:57
  73.0 3.3 %all-to-all-done.1 = f32[1,780,192]{1,0,2:T(1,128)S(1)} async-done(((f32[1,780,192]{1,0,2:T(1,128)}), f32[1,780,192]{1,0,2:T(1,128)S(1)}, u32[]{:S(2)}, u32[]{:S(2)}) %all-to-all-start.1) | async-done | bytes 599072 | tf_op jit(solution)/shard_map/all_to_all | solution.py:209
  76.3 1.9 %copy.363 = f32[64,1,780,3]{0,2,3,1:T(8,128)} copy(f32[64,1,780,3]{2,1,3,0:T(1,128)S(1)} %bitcast.100) | data formatting | bytes 1198080 | tf_op jit(solution)/shard_map/all_to_all | solution.py:209
  78.2 1.5 %reshape.478 = f32[64,3,2,26,5,3]{0,4,3,2,1,5:T(8,128)S(1)} reshape(f32[64,1,780,3]{0,2,3,1:T(8,128)} %copy.363) | data formatting | bytes 1198080 | tf_op jit(solution)/shard_map/reshape | solution.py:212
  79.6 4.6 %copy.364 = f32[3,3,2,26,64,5]{3,2,5,4,1,0:T(2,128)} copy(f32[3,3,2,26,64,5]{4,5,3,2,1,0:T(8,128)S(1)} %bitcast.92) | data formatting | bytes 1198080 | tf_op jit(solution)/shard_map/transpose | solution.py:213
  84.2 4.5 %copy.365 = f32[3,3,2,26,320]{4,3,2,1,0:T(8,128)S(1)} copy(f32[3,3,2,26,320]{3,2,4,1,0:T(2,128)} %bitcast.91) | data formatting | bytes 1198080 | tf_op jit(solution)/shard_map/reshape | solution.py:214
  89.3 0.5 copy-done.10
  89.9 0.4 select_maximum_fusion.8
  90.2 0.6 fusion.55
  91.9 0.6 fusion.49
  92.8 0.4 fusion.16
  93.7 0.6 fusion.43
  94.6 0.5 fusion.18
  95.2 0.4 select_maximum_fusion.2
  95.6 0.6 fusion.37
  96.6 0.6 fusion.20
  97.6 0.6 fusion.31
  98.6 0.5 copy-done.11
  99.1 0.9 broadcast_select_fusion
  100.0 1.2 copy.367
  101.2 8.3 %all-to-all-start.2 = ((f32[1,288,320]{1,0,2:T(1,128)}), f32[1,288,320]{1,0,2:T(1,128)S(1)}, u32[]{:S(2)}, u32[]{:S(2)}) async-start(f32[1,288,320]{1,0,2:T(1,128)} %copy.367), calls=%async_computation.2 | async-start | bytes 983040 | tf_op jit(solution)/shard_map/all_to_all | solution.py:228
  109.9 0.8 copy.348
  110.9 15.5 %all-to-all-done.2 = f32[1,288,320]{1,0,2:T(1,128)S(1)} async-done(((f32[1,288,320]{1,0,2:T(1,128)}), f32[1,288,320]{1,0,2:T(1,128)S(1)}, u32[]{:S(2)}, u32[]{:S(2)}) %all-to-all-start.2) | async-done | bytes 368672 | tf_op jit(solution)/shard_map/all_to_all | solution.py:228
  126.5 3.0 %reshape.481 = f32[192,2,3,16,5]{3,2,1,0,4:T(4,128)} reshape(f32[64,1,288,5]{2,0,3,1:T(8,128)S(1)} %copy.368) | data formatting | bytes 737280 | tf_op jit(solution)/shard_map/reshape | solution.py:229
  129.5 5.2 %fusion.5 = f32[3,16,5,128]{3,1,2,0:T(8,128)} fusion(f32[192,2,3,16,5]{3,2,1,0,4:T(4,128)} %reshape.481, f32[128,192,1]{0,1,2:T(8,128)S(1)} %get-tuple-element.94, f32[128,192,1]{0,1,2:T(8,128)S(1)} %get-tuple-element.98, f32[128,3,16,5]{0,2,3,1:T(8,128)S(1)} %copy.349, f32[192]{0:T(256)S(1)} %reshape.486, f32[128]{0:T(128)S(1)} %exponential_multiply_fusion), kind=kOutput, calls=%fused_computation.8 | convolution fusion | flops 70957056 | bytes 812288 | tf_op jit(solution)/shard_map/spfyx,tsp->fyxt/dot_general | solution.py:232
  (89 shorter events, 8.3 us)
Async XLA Ops:
  0.6 8.3 %copy-start.9 = (s32[64,3]{0,1:T(4,128)S(1)}, s32[64,3]{0,1:T(4,128)}, u32[]{:S(2)}) copy-start(s32[64,3]{0,1:T(4,128)} %param.12) | copy-start | bytes 2308
  1.7 9.8 %collective-permute-start.1 = (f32[16,6,320]{2,1,0:T(8,128)S(1)}, f32[16,6,320]{2,1,0:T(8,128)S(1)}, u32[]{:S(2)}, u32[]{:S(2)}) collective-permute-start(f32[16,6,320]{2,1,0:T(8,128)S(1)} %get-tuple-element.85), channel_id=1, source_target_pairs={{1,0},{2,1},{3,2},{4,3},{5,4},{6,5},{7,6},{9,8},{10,9},{11,10},{12... | collective-permute-start | bytes 368648 | tf_op jit(solution)/shard_map/ppermute | solution.py:142
  3.7 8.8 %collective-permute-start = (f32[16,6,320]{2,1,0:T(8,128)S(1)}, f32[16,6,320]{2,1,0:T(8,128)S(1)}, u32[]{:S(2)}, u32[]{:S(2)}) collective-permute-start(f32[16,6,320]{2,1,0:T(8,128)S(1)} %get-tuple-element.86), channel_id=1, source_target_pairs={{0,1},{1,2},{2,3},{3,4},{4,5},{5,6},{6,7},{8,9},{9,10},{10,11},{11... | collective-permute-start | bytes 368648 | tf_op jit(solution)/shard_map/ppermute | solution.py:141
  13.4 13.0 %copy-start.12 = (s32[64]{0:T(128)S(1)}, s32[64]{0:T(128)}, u32[]{:S(2)}) copy-start(s32[64]{0:T(128)} %param.13) | copy-start | bytes 772
  13.4 14.1 %copy-start.4 = (f32[2,3,16,320]{3,2,1,0:T(8,128)S(1)}, f32[2,3,16,320]{3,2,1,0:T(8,128)}, u32[]{:S(2)}) copy-start(f32[2,3,16,320]{3,2,1,0:T(8,128)} %param.8) | copy-start | bytes 368644
  13.4 14.1 %copy-start.5 = (f32[2,3,16,320]{3,2,1,0:T(8,128)S(1)}, f32[2,3,16,320]{3,2,1,0:T(8,128)}, u32[]{:S(2)}) copy-start(f32[2,3,16,320]{3,2,1,0:T(8,128)} %param.7) | copy-start | bytes 368644
  13.4 14.1 %copy-start.6 = (f32[3,16,320]{2,1,0:T(8,128)S(1)}, f32[3,16,320]{2,1,0:T(8,128)}, u32[]{:S(2)}) copy-start(f32[3,16,320]{2,1,0:T(8,128)} %param.9) | copy-start | bytes 184324
  13.4 14.1 %copy-start.8 = (f32[16,320]{1,0:T(8,128)S(1)}, f32[16,320]{1,0:T(8,128)}, u32[]{:S(2)}) copy-start(f32[16,320]{1,0:T(8,128)} %param.10) | copy-start | bytes 61444
  14.7 28.7 %all-to-all-start = ((f32[1,3,94,320]{2,0,1,3:T(1,128)}), f32[1,3,94,320]{2,0,1,3:T(1,128)S(1)}, u32[]{:S(2)}, u32[]{:S(2)}) async-start(f32[1,3,94,320]{2,0,1,3:T(1,128)} %copy.345), calls=%async_computation | async-start | bytes 983040 | tf_op jit(solution)/shard_map/all_to_all | solution.py:183
  47.6 7.7 %copy-start = (f32[3,3,2,16,320]{4,3,2,1,0:T(8,128)S(1)}, f32[3,3,2,16,320]{4,3,2,1,0:T(8,128)}, u32[]{:S(2)}) copy-start(f32[3,3,2,16,320]{4,3,2,1,0:T(8,128)} %param.11) | copy-start | bytes 1105924
  49.5 26.7 %all-to-all-start.1 = ((f32[1,780,192]{1,0,2:T(1,128)}), f32[1,780,192]{1,0,2:T(1,128)S(1)}, u32[]{:S(2)}, u32[]{:S(2)}) async-start(f32[1,780,192]{1,0,2:T(1,128)} %copy.362), calls=%async_computation.1 | async-start | bytes 1376256 | tf_op jit(solution)/shard_map/all_to_all | solution.py:209
  55.4 9.7 %collective-permute-start.2 = (f32[18,6,320]{2,0,1:T(8,128)S(1)}, f32[18,6,320]{2,0,1:T(8,128)S(1)}, u32[]{:S(2)}, u32[]{:S(2)}) collective-permute-start(f32[18,6,320]{2,0,1:T(8,128)S(1)} %copy.381), channel_id=1, source_target_pairs={{0,1},{1,2},{2,3},{3,4},{4,5},{5,6},{6,7},{8,9},{9,10},{10,11},{11... | collective-permute-start | bytes 414728 | tf_op jit(solution)/shard_map/ppermute | solution.py:141
  60.7 9.3 %collective-permute-start.3 = (f32[18,6,320]{2,0,1:T(8,128)S(1)}, f32[18,6,320]{2,0,1:T(8,128)S(1)}, u32[]{:S(2)}, u32[]{:S(2)}) collective-permute-start(f32[18,6,320]{2,0,1:T(8,128)S(1)} %copy.382), channel_id=1, source_target_pairs={{1,0},{2,1},{3,2},{4,3},{5,4},{6,5},{7,6},{9,8},{10,9},{11,10},{12... | collective-permute-start | bytes 414728 | tf_op jit(solution)/shard_map/ppermute | solution.py:142
  84.2 4.6 %copy-start.1 = (f32[3,1,2,32,320]{4,3,2,1,0:T(8,128)S(1)}, f32[3,1,2,32,320]{4,3,2,1,0:T(8,128)}, u32[]{:S(2)}) copy-start(f32[3,1,2,32,320]{4,3,2,1,0:T(8,128)} %get-tuple-element.35) | copy-start | bytes 737284
  84.2 4.6 %copy-start.2 = (f32[3,1,2,32,320]{4,3,2,1,0:T(8,128)S(1)}, f32[3,1,2,32,320]{4,3,2,1,0:T(8,128)}, u32[]{:S(2)}) copy-start(f32[3,1,2,32,320]{4,3,2,1,0:T(8,128)} %get-tuple-element.36) | copy-start | bytes 737284
  84.2 4.6 %copy-start.3 = (f32[3,1,2,32,320]{4,3,2,1,0:T(8,128)S(1)}, f32[3,1,2,32,320]{4,3,2,1,0:T(8,128)}, u32[]{:S(2)}) copy-start(f32[3,1,2,32,320]{4,3,2,1,0:T(8,128)} %get-tuple-element.44) | copy-start | bytes 737284
  89.1 0.6 copy-start.10
  98.4 0.7 copy-start.11
  100.0 9.4 %copy-start.7 = (f32[64,3]{1,0:T(8,128)S(1)}, f32[64,3]{1,0:T(8,128)}, u32[]{:S(2)}) copy-start(f32[64,3]{1,0:T(8,128)} %get-tuple-element.101) | copy-start | bytes 2308
  101.2 25.3 %all-to-all-start.2 = ((f32[1,288,320]{1,0,2:T(1,128)}), f32[1,288,320]{1,0,2:T(1,128)S(1)}, u32[]{:S(2)}, u32[]{:S(2)}) async-start(f32[1,288,320]{1,0,2:T(1,128)} %copy.367), calls=%async_computation.2 | async-start | bytes 983040 | tf_op jit(solution)/shard_map/all_to_all | solution.py:228
